TPU v7x, 128 devices: a whole 4x4x4 slice. The times are simulated.
128 devices in a mesh: seq: 32 (over z, x, y_lo), type: 4 (over y_hi, core).
Axes of the slice: x: 4, y: 4 (y_hi: 2, y_lo: 2; y = y_hi * 2 + y_lo), z: 4, core: 2. Of those that a mesh axis runs over, the one named last changes fastest.
Arguments:
- tokens: bfloat16 [17408, 1024], P(('seq', 'type')), may hold values from -60 to 60
- shift_scale: float32 [2, 1024], replicated, may hold values from -0.8 to 0.8
- branch_gate: float32 [1024], replicated, may hold values from 0.25 to 1.75
- final_gain: float32 [1024], replicated, may hold values from 0.5 to 1.5
- w_qkv: bfloat16 [3, 1024, 1024], P(None, None, 'type'), may hold values from -1 to 1
- w_out: bfloat16 [1024, 1024], P('type'), may hold values from -0.375 to 0.375
- type_ids: int32 [17408, 1], P(('seq', 'type')), may hold values from 0 to 7; in each aligned block of 136 rows (0 to 135, 136 to 271, ...) at most 51 rows name the same one
- head_w1: bfloat16 [8, 1024, 1024], P('type'), may hold values from -0.1875 to 0.1875
- head_b1: bfloat16 [8, 1024], P('type'), may hold values from -3 to 3
- head_w2: bfloat16 [8, 1024, 16], P('type'), may hold values from -0.1875 to 0.1875
Outputs:
- updated: bfloat16 [17408, 1024], P(('seq', 'type'))
- head_out: float32 [17408, 16], P(('seq', 'type'))
Inputs may be any that keep to these rules, and one draw needn't show every extreme that they name: `type_ids`: among the 136 tokens of one device no type occurs more than 51 times; some type occurs exactly 51 times on some devices.
All inputs are finite; a program needn't handle non-finite values.
Results may differ from a plain program's by a relative error of at most 0.014.
Values may be sent and summed in bfloat16 or wider, within the bound.
No kernel may reach another device: no remote copies, remote signals or barrier semaphores. Data moves between devices by JAX's collectives and lax.ppermute only.
A program may use at most 192 MiB of HBM per device.

v0:
```python
import jax
import jax.numpy as jnp
from jax import lax
from jax.sharding import PartitionSpec as P

HD = 64


def rms_normalize(values):
    squares = jnp.mean(values * values, axis=-1, keepdims=True)
    return values * lax.rsqrt(squares + 1e-06)


def absorb_block(state, query_heads, key_heads, value_heads):
    largest, totals, numer = state
    scores = jnp.einsum(
        "qhd,khd->hqk", query_heads, key_heads, preferred_element_type=jnp.float32
    ) * HD ** (-0.5)
    newmax = jnp.maximum(largest, jnp.max(scores, axis=-1))
    decay = jnp.exp(largest - newmax)
    weights = jnp.exp(scores - newmax[:, :, None])
    totals = totals * decay + jnp.sum(weights, axis=-1)
    update = jnp.einsum(
        "hqk,khd->qhd",
        weights.astype(jnp.bfloat16),
        value_heads,
        preferred_element_type=jnp.float32,
    )
    numer = numer * jnp.transpose(decay)[:, :, None] + update
    return (newmax, totals, numer)


def apply_heads(feature_slots, first_w, first_b, second_w):
    hidden = jnp.einsum(
        "...tcd,tdh->...tch", feature_slots, first_w, preferred_element_type=jnp.float32
    )
    hidden = jax.nn.gelu(hidden + first_b.astype(jnp.float32)[:, None, :]).astype(jnp.bfloat16)
    return jnp.einsum("...tch,tho->...tco", hidden, second_w, preferred_element_type=jnp.float32)


def body(
    tokens, shift_scale, branch_gate, final_gain, w_qkv, w_out, type_ids, head_w1, head_b1, head_w2
):
    inputs = tokens.astype(jnp.float32)
    modulated = (rms_normalize(inputs) * (1.0 + shift_scale[1]) + shift_scale[0]).astype(
        jnp.bfloat16
    )
    projected = jnp.einsum(
        "rd,ide->ire",
        lax.all_gather(modulated, "type", axis=0, tiled=True),
        w_qkv,
        preferred_element_type=jnp.float32,
    ).astype(jnp.bfloat16)
    queries = projected[0]
    local_keys = projected[1]
    local_values = projected[2]
    query_count = queries.shape[0]
    width = queries.shape[1]
    local_heads = width // HD
    query_heads = queries.reshape(query_count, local_heads, HD)
    initial = (
        jnp.full((local_heads, query_count), -1e30, jnp.float32),
        jnp.zeros((local_heads, query_count), jnp.float32),
        jnp.zeros((query_count, local_heads, HD), jnp.float32),
    )
    running = initial
    key_part = lax.all_gather(local_keys, "seq", axis=0, tiled=True)
    value_part = lax.all_gather(local_values, "seq", axis=0, tiled=True)
    row_total = key_part.shape[0]
    key_blocks = key_part.reshape(row_total // 512, 512, local_heads, HD)
    value_blocks = value_part.reshape(row_total // 512, 512, local_heads, HD)

    def advance(state, pair):
        return (absorb_block(state, query_heads, pair[0], pair[1]), None)

    running, unused = lax.scan(advance, running, (key_blocks, value_blocks))
    largest, totals, numer = running
    attended = (
        (numer / jnp.transpose(totals)[:, :, None]).astype(jnp.bfloat16).reshape(query_count, width)
    )
    mixed = lax.psum_scatter(
        jnp.dot(attended, w_out, preferred_element_type=jnp.float32),
        "type",
        scatter_dimension=0,
        tiled=True,
    )
    updated = (inputs + branch_gate * mixed).astype(jnp.bfloat16)
    final = (rms_normalize(updated.astype(jnp.float32)) * final_gain).astype(jnp.bfloat16)
    owned = head_w1.shape[0]
    owners = lax.axis_size("type")
    kinds_all = owned * owners
    capacity = 3 * tokens.shape[0] // 8
    kinds = type_ids[:, 0]
    onehot = (kinds[:, None] == jnp.arange(kinds_all, dtype=jnp.int32)[None, :]).astype(jnp.int32)
    ranks = jnp.sum((jnp.cumsum(onehot, axis=0) - onehot) * onehot, axis=1)
    slots = kinds * capacity + ranks
    slot_ids = jnp.arange(kinds_all * capacity, dtype=jnp.int32)
    dispatch = (slot_ids[:, None] == slots[None, :]).astype(jnp.bfloat16)
    packed = jnp.dot(dispatch, final, preferred_element_type=jnp.float32).astype(jnp.bfloat16)
    packed = packed.reshape(kinds_all, capacity, final.shape[1])
    first_w, first_b, second_w = (
        lax.all_gather(head_w1, "type", axis=0, tiled=True),
        lax.all_gather(head_b1, "type", axis=0, tiled=True),
        lax.all_gather(head_w2, "type", axis=0, tiled=True),
    )
    answers = apply_heads(packed, first_w, first_b, second_w)
    answers = answers.reshape(kinds_all * capacity, head_w2.shape[2])
    gather_back = (slots[:, None] == slot_ids[None, :]).astype(jnp.float32)
    head_out = jnp.dot(
        gather_back, answers, precision=lax.Precision.HIGHEST, preferred_element_type=jnp.float32
    )
    return (updated, head_out)


def solution(mesh):
    in_specs = (
        P(("seq", "type"), None),
        P(),
        P(),
        P(),
        P(None, None, "type"),
        P("type", None),
        P(("seq", "type"), None),
        P("type", None, None),
        P("type", None),
        P("type", None, None),
    )
    out_specs = (P(("seq", "type"), None), P(("seq", "type"), None))
    return jax.shard_map(body, mesh=mesh, in_specs=in_specs, out_specs=out_specs, check_vma=False)
```

profile of v0, /device:TPU:1, one launch (start us, length us, event | category | flops | bytes accessed | tf_op | source)
XLA Modules:
  0.0 957.8 jit_solution(635125774649194052)
XLA Ops:
  11.1 24.9 %all-gather.8.cloned.1.call-done = bf16[544,1024]{1,0:T(8,128)(2,1)} async-done(((bf16[136,1024]{1,0:T(8,128)(2,1)}), bf16[544,1024]{1,0:T(8,128)(2,1)}) %all-gather.8.cloned.1.call-update) | async-done | bytes 1114128 | tf_op jit(solution)/shard_map/all_gather | solution.py:50
  40.1 196.5 %all-gather.12.cloned.1.call-done = bf16[1,17408,256]{2,1,0:T(8,128)(2,1)} async-done(((bf16[1,544,256]{2,1,0:T(8,128)(2,1)}), bf16[1,17408,256]{2,1,0:T(8,128)(2,1)}) %all-gather.12.cloned.1.call-update) | async-done | bytes 8912912 | tf_op jit(solution)/shard_map/all_gather | solution.py:67
  236.6 25.9 %reshape.77 = bf16[34,512,4,64]{3,2,1,0:T(4,128)(2,1)} reshape(bf16[1,17408,256]{2,1,0:T(8,128)(2,1)} %all-gather.12.cloned.1.call-done) | data formatting | bytes 17825792 | tf_op jit(solution)/shard_map/reshape | solution.py:70
  262.5 25.6 %copy.24 = bf16[34,512,4,64]{1,3,2,0:T(8,128)(2,1)} copy(bf16[34,512,4,64]{3,2,1,0:T(4,128)(2,1)} %reshape.77) | data formatting | bytes 17825792
  288.2 150.6 %all-gather.14.cloned.1.call-done = bf16[1,17408,256]{2,1,0:T(8,128)(2,1)} async-done(((bf16[1,544,256]{2,1,0:T(8,128)(2,1)}), bf16[1,17408,256]{2,1,0:T(8,128)(2,1)}) %all-gather.14.cloned.1.call-update) | async-done | bytes 8912912 | tf_op jit(solution)/shard_map/all_gather | solution.py:68
  438.8 25.9 %reshape.78 = bf16[34,512,4,64]{3,2,1,0:T(4,128)(2,1)} reshape(bf16[1,17408,256]{2,1,0:T(8,128)(2,1)} %all-gather.14.cloned.1.call-done) | data formatting | bytes 17825792 | tf_op jit(solution)/shard_map/reshape | solution.py:71
  464.7 25.6 %copy.25 = bf16[34,512,4,64]{1,3,2,0:T(8,128)(2,1)} copy(bf16[34,512,4,64]{3,2,1,0:T(4,128)(2,1)} %reshape.78) | data formatting | bytes 17825792
  490.3 298.6 %while.15 = (s32[]{:T(128)}, f32[4,544]{1,0:T(4,128)S(1)}, f32[4,544]{1,0:T(4,128)S(1)}, f32[544,4,64]{0,2,1:T(8,128)S(1)}, bf16[34,512,4,64]{1,3,2,0:T(8,128)(2...) while((s32[]{:T(128)}, f32[4,544]{1,0:T(4,128)S(1)}, ...), condition=%wide.region_4.5_spmd.clone, body=%wide.region_1.4_spmd.clone.sunk | while | flops 294556416 | bytes 33252484 | solution.py:76
  490.3 3.8 bitcast_reduce_fusion.2
  499.2 3.8 bitcast_reduce_fusion.2
  507.9 3.8 bitcast_reduce_fusion.2
  511.7 3.6 fusion.83
  516.7 3.8 bitcast_reduce_fusion.2
  525.5 3.8 bitcast_reduce_fusion.2
  534.3 3.8 bitcast_reduce_fusion.2
  543.1 3.8 bitcast_reduce_fusion.2
  551.9 3.8 bitcast_reduce_fusion.2
  560.6 3.8 bitcast_reduce_fusion.2
  569.4 3.8 bitcast_reduce_fusion.2
  578.2 3.8 bitcast_reduce_fusion.2
  587.0 3.8 bitcast_reduce_fusion.2
  595.8 3.8 bitcast_reduce_fusion.2
  604.5 3.8 bitcast_reduce_fusion.2
  613.3 3.8 bitcast_reduce_fusion.2
  622.1 3.8 bitcast_reduce_fusion.2
  630.9 3.8 bitcast_reduce_fusion.2
  639.7 3.8 bitcast_reduce_fusion.2
  648.4 3.8 bitcast_reduce_fusion.2
  657.2 3.8 bitcast_reduce_fusion.2
  666.0 3.8 bitcast_reduce_fusion.2
  674.8 3.8 bitcast_reduce_fusion.2
  683.6 3.8 bitcast_reduce_fusion.2
  692.4 3.8 bitcast_reduce_fusion.2
  701.1 3.8 bitcast_reduce_fusion.2
  709.9 3.8 bitcast_reduce_fusion.2
  718.7 3.8 bitcast_reduce_fusion.2
  727.5 3.8 bitcast_reduce_fusion.2
  736.3 3.8 bitcast_reduce_fusion.2
  745.0 3.8 bitcast_reduce_fusion.2
  753.8 3.8 bitcast_reduce_fusion.2
  762.6 3.8 bitcast_reduce_fusion.2
  771.4 3.8 bitcast_reduce_fusion.2
  780.2 3.8 bitcast_reduce_fusion.2
  792.4 11.0 %all-gather.2 = bf16[4,2,1024]{2,1,0:T(2,128)(2,1)S(1)} all-gather(bf16[1,2,1024]{2,1,0:T(2,128)(2,1)S(1)} %bitcast.83), channel_id=1, replica_groups=mesh['seq'=32,'type'=4] {'type'}, dimensions={0}, use_global_device_ids=true | all-gather | bytes 20480 | tf_op jit(solution)/shard_map/all_gather | solution.py:103
  803.5 7.4 all_gather.23
  811.0 20.2 %reduce-scatter.2.cloned.1.call-done = f32[136,1024]{1,0:T(8,128)} async-done(((f32[544,1024]{1,0:T(8,128)}), f32[136,1024]{1,0:T(8,128)}) %reduce-scatter.2.cloned.1.call-update) | async-done | bytes 557072 | tf_op jit(solution)/shard_map/reduce_scatter | solution.py:81
  833.3 109.4 %all-gather.10.cloned.1.call-done = bf16[8,1024,1024]{2,1,0:T(8,128)(2,1)} async-done(((bf16[2,1024,1024]{2,1,0:T(8,128)(2,1)}), bf16[8,1024,1024]{2,1,0:T(8,128)(2,1)}) %all-gather.10.cloned.1.call-update) | async-done | bytes 16777232 | tf_op jit(solution)/shard_map/all_gather | solution.py:102
  942.7 7.6 fusion.32
  (297 shorter events, 179.9 us)
Async XLA Ops:
  7.2 28.8 %copy-start = (bf16[3,1024,256]{2,1,0:T(8,128)(2,1)S(1)}, bf16[3,1024,256]{2,1,0:T(8,128)(2,1)}, u32[]{:S(2)}) copy-start(bf16[3,1024,256]{2,1,0:T(8,128)(2,1)} %param.16) | copy-start | bytes 4718596
  7.2 28.7 %all-gather.8.cloned.1.call-start = ((), (), s32[]{:S(2)}) async-start(), calls=%async_computation.1 | async-start | bytes 1392640 | tf_op jit(solution)/shard_map/all_gather | solution.py:50
  11.0 225.6 %all-gather.12.cloned.1.call-start = ((), (), s32[]{:S(2)}) async-start(), calls=%async_computation.4 | async-start | bytes 9191424 | tf_op jit(solution)/shard_map/all_gather | solution.py:67
  39.1 399.7 %all-gather.14.cloned.1.call-start = ((), (), s32[]{:S(2)}) async-start(), calls=%async_computation.5 | async-start | bytes 9191424 | tf_op jit(solution)/shard_map/all_gather | solution.py:68
  39.8 791.4 %reduce-scatter.2.cloned.1.call-start = ((), (), s32[]{:S(2)}) async-start(), calls=%async_computation.2 | async-start | bytes 2785280 | tf_op jit(solution)/shard_map/reduce_scatter | solution.py:81
  490.3 298.7 %copy-start.5 = (bf16[256,1024]{1,0:T(8,128)(2,1)S(1)}, bf16[256,1024]{1,0:T(8,128)(2,1)}, u32[]{:S(2)}) copy-start(bf16[256,1024]{1,0:T(8,128)(2,1)} %param.17) | copy-start | bytes 1572868
  494.2 3.7 copy-start.2
  502.9 3.7 copy-start.2
  511.7 3.7 copy-start.2
  520.5 3.7 copy-start.2
  529.3 3.7 copy-start.2
  538.1 3.7 copy-start.2
  546.8 3.7 copy-start.2
  555.6 3.7 copy-start.2
  564.4 3.7 copy-start.2
  573.2 3.7 copy-start.2
  582.0 3.7 copy-start.2
  590.7 3.7 copy-start.2
  599.5 3.7 copy-start.2
  608.3 3.7 copy-start.2
  617.1 3.7 copy-start.2
  625.9 3.7 copy-start.2
  634.7 3.7 copy-start.2
  643.4 3.7 copy-start.2
  652.2 3.7 copy-start.2
  661.0 3.7 copy-start.2
  669.8 3.7 copy-start.2
  678.6 3.7 copy-start.2
  687.3 3.7 copy-start.2
  696.1 3.7 copy-start.2
  704.9 3.7 copy-start.2
  713.7 3.7 copy-start.2
  722.5 3.7 copy-start.2
  731.3 3.7 copy-start.2
  740.0 3.7 copy-start.2
  748.8 3.7 copy-start.2
  757.6 3.7 copy-start.2
  766.4 3.7 copy-start.2
  775.2 3.7 copy-start.2
  783.9 3.7 copy-start.2
  789.0 3.4 copy-start.10
  789.0 14.4 %copy-start.6 = (bf16[2,1024,16]{1,2,0:T(8,128)(2,1)S(1)}, bf16[2,1024,16]{1,2,0:T(8,128)(2,1)}, u32[]{:S(2)}) copy-start(bf16[2,1024,16]{1,2,0:T(8,128)(2,1)} %param.21) | copy-start | bytes 196612
  789.1 42.2 %copy-start.3 = (bf16[136,1024]{1,0:T(8,128)(2,1)S(1)}, bf16[136,1024]{1,0:T(8,128)(2,1)}, u32[]{:S(2)}) copy-start(bf16[136,1024]{1,0:T(8,128)(2,1)} %param.12) | copy-start | bytes 835588
  789.1 42.2 %copy-start.8 = (f32[1024]{0:T(1024)S(1)}, f32[1024]{0:T(1024)}, u32[]{:S(2)}) copy-start(f32[1024]{0:T(1024)} %param.14) | copy-start | bytes 12292
  790.9 41.6 %copy-start.9 = (f32[1024]{0:T(1024)S(1)}, f32[1024]{0:T(1024)}, u32[]{:S(2)}) copy-start(f32[1024]{0:T(1024)} %param.15) | copy-start | bytes 12292
  791.0 151.7 %all-gather.10.cloned.1.call-start = ((), (), s32[]{:S(2)}) async-start(), calls=%async_computation.3 | async-start | bytes 20971520 | tf_op jit(solution)/shard_map/all_gather | solution.py:102
  832.5 117.8 %copy-start.4 = (bf16[136,1024]{1,0:T(8,128)(2,1)}, bf16[136,1024]{1,0:T(8,128)(2,1)S(1)}, u32[]{:S(2)}) copy-start(bf16[136,1024]{1,0:T(8,128)(2,1)S(1)} %get-tuple-element.104) | copy-start | bytes 835588
  942.7 8.6 copy-start.1
  (1 other events, 2.5 us)
Sparse Core Ops, SparseCore 0:
  11.1 24.7 all-gather.7
  39.2 197.3 all-gather.11
  238.8 199.9 all-gather.13
  791.1 40.1 reduce-scatter.1
  832.8 109.7 all-gather.9
where the time goes:
time: 962 us; the launch traced here: 958 us
  waiting for transfers between devices  503 us (52%)
  matrix products  264 us (27%)
  local copies, waits for them, and re-layouts  106 us (11%)
  other arithmetic  50.4 us (5%)
  blocking collectives  18.4 us (2%)
  between operations  14 us (1%)
    all_gather x1, waiting for transfers between devices, body(): key_part = lax.all_gather(local_keys, 'seq', axis=0, tiled=True)  197 us
    all_gather x1, waiting for transfers between devices, body(): value_part = lax.all_gather(local_values, 'seq', axis=0, tiled=True)  151 us
    dot_general x34, matrix products, absorb_block(): jnp.einsum('qhd,khd->hqk', query_heads, key_heads, preferred_element_type...  128 us
    dot_general x34, matrix products, absorb_block(): jnp.einsum('hqk,khd->qhd', weights.astype(jnp.bfloat16), value_heads, pre...  123 us
    all_gather x1, waiting for transfers between devices, body(): lax.all_gather(head_w1, 'type', axis=0, tiled=True)  109 us
    unnamed x22, local copies, waits for them, and re-layouts  51.3 us
    reduce_sum x34, other arithmetic, absorb_block(): totals = totals * decay + jnp.sum(weights, axis=-1)  43.5 us
    reshape x1, local copies, waits for them, and re-layouts, body(): key_blocks = key_part.reshape(row_total // 512, 512, local_heads, HD)  25.9 us
  transfers between devices with their start and end apart: 5, of which 5 were waited for; matrix products, arithmetic and copies ran while one was open for 6% of the time, Pallas kernels for 0%

commit v1 on v0

--- a/solution.py
+++ b/solution.py
@@ -65,7 +65,10 @@
     )
     running = initial
     key_part = lax.all_gather(local_keys, "seq", axis=0, tiled=True)
-    value_part = lax.all_gather(local_values, "seq", axis=0, tiled=True)
+    size = lax.axis_size("seq")
+    blocks = jnp.stack([local_values for _ in range(size)])
+    blocks = lax.all_to_all(blocks, "seq", split_axis=0, concat_axis=0)
+    value_part = jnp.concatenate(blocks, axis=0)
     row_total = key_part.shape[0]
     key_blocks = key_part.reshape(row_total // 512, 512, local_heads, HD)
     value_blocks = value_part.reshape(row_total // 512, 512, local_heads, HD)

time: 962 us -> 881 us (0.916)
  waiting for transfers between devices: 503 us -> 412 us
    all_gather x1 -> x0, waiting for transfers between devices: 151 us -> none  [body(): value_part = lax.all_gather(local_values, 'seq', axis=0, tiled=True)]
    all_to_all x0 -> x1, waiting for transfers between devices: none -> 145 us  [body(): blocks = lax.all_to_all(blocks, 'seq', split_axis=0, concat_axis=0)]
    all_gather x1, waiting for transfers between devices: 197 us -> 112 us  [body(): key_part = lax.all_gather(local_keys, 'seq', axis=0, tiled=True)]
    another operation x1 -> x3, local copies, waits for them, and re-layouts: 0.01 us -> 30.4 us  [the longest x1 25.9 us: body(): value_blocks = value_part.reshape(row_total // 512, 512, local_heads, HD)]
    reshape x1 -> x0, local copies, waits for them, and re-layouts: 25.9 us -> none  [body(): value_blocks = value_part.reshape(row_total // 512, 512, local_heads, HD)]
  transfers between devices with their start and end apart: 5 -> 5, of which waited for: 5 -> 5; matrix products, arithmetic and copies ran while one was open for 6% -> 7% of each run, Pallas kernels for 0% -> 0%
where the time goes in v1:
time: 881 us; the launch traced here: 877 us
  waiting for transfers between devices  412 us (47%)
  matrix products  264 us (30%)
  local copies, waits for them, and re-layouts  111 us (13%)
  other arithmetic  50.4 us (6%)
  blocking collectives  16.9 us (2%)
  between operations  14 us (2%)
    all_to_all x1, waiting for transfers between devices, body(): blocks = lax.all_to_all(blocks, 'seq', split_axis=0, concat_axis=0)  145 us
    dot_general x34, matrix products, absorb_block(): jnp.einsum('qhd,khd->hqk', query_heads, key_heads, preferred_element_type...  128 us
    dot_general x34, matrix products, absorb_block(): jnp.einsum('hqk,khd->qhd', weights.astype(jnp.bfloat16), value_heads, pre...  123 us
    all_gather x1, waiting for transfers between devices, body(): key_part = lax.all_gather(local_keys, 'seq', axis=0, tiled=True)  112 us
    all_gather x1, waiting for transfers between devices, body(): lax.all_gather(head_w1, 'type', axis=0, tiled=True)  109 us
    unnamed x22, local copies, waits for them, and re-layouts  51.3 us
    reduce_sum x34, other arithmetic, absorb_block(): totals = totals * decay + jnp.sum(weights, axis=-1)  43.5 us
    another operation x1, local copies, waits for them, and re-layouts, body(): value_blocks = value_part.reshape(row_total // 512, 512, local_heads, HD)  25.9 us
  transfers between devices with their start and end apart: 5, of which 5 were waited for; matrix products, arithmetic and copies ran while one was open for 7% of the time, Pallas kernels for 0%

profile of v1, /device:TPU:1, one launch (start us, length us, event | category | flops | bytes accessed | tf_op | source)
XLA Modules:
  0.0 877.3 jit_solution(10209492818713163507)
XLA Ops:
  11.1 24.9 %all-gather.6.cloned.1.call-done = bf16[544,1024]{1,0:T(8,128)(2,1)} async-done(((bf16[136,1024]{1,0:T(8,128)(2,1)}), bf16[544,1024]{1,0:T(8,128)(2,1)}) %all-gather.6.cloned.1.call-update) | async-done | bytes 1114128 | tf_op jit(solution)/shard_map/all_gather | solution.py:50
  39.0 4.4 stack.3
  43.4 7.1 all-to-all-start
  50.8 145.0 %all-to-all-done = bf16[32,544,256]{2,1,0:T(8,128)(2,1)} async-done(((bf16[32,544,256]{2,1,0:T(8,128)(2,1)}), bf16[32,544,256]{2,1,0:T(8,128)(2,1)}, u32[]{:S(2)}, u32[]{:S(2)}) %all-to-all-start) | async-done | bytes 8912928 | tf_op jit(solution)/shard_map/all_to_all | solution.py:70
  195.8 25.9 %reshape.73 = bf16[34,512,4,64]{3,2,1,0:T(4,128)(2,1)} reshape(bf16[32,544,256]{2,1,0:T(8,128)(2,1)} %all-to-all-done) | data formatting | bytes 17825792 | tf_op jit(solution)/shard_map/reshape;reshape | solution.py:74
  221.8 25.6 %copy.24 = bf16[34,512,4,64]{1,3,2,0:T(8,128)(2,1)} copy(bf16[34,512,4,64]{3,2,1,0:T(4,128)(2,1)} %reshape.73) | data formatting | bytes 17825792
  247.4 111.7 %all-gather.10.cloned.1.call-done = bf16[1,17408,256]{2,1,0:T(8,128)(2,1)} async-done(((bf16[1,544,256]{2,1,0:T(8,128)(2,1)}), bf16[1,17408,256]{2,1,0:T(8,128)(2,1)}) %all-gather.10.cloned.1.call-update) | async-done | bytes 8912912 | tf_op jit(solution)/shard_map/all_gather | solution.py:67
  359.1 25.9 %reshape.72 = bf16[34,512,4,64]{3,2,1,0:T(4,128)(2,1)} reshape(bf16[1,17408,256]{2,1,0:T(8,128)(2,1)} %all-gather.10.cloned.1.call-done) | data formatting | bytes 17825792 | tf_op jit(solution)/shard_map/reshape | solution.py:73
  385.0 25.6 %copy.23 = bf16[34,512,4,64]{1,3,2,0:T(8,128)(2,1)} copy(bf16[34,512,4,64]{3,2,1,0:T(4,128)(2,1)} %reshape.72) | data formatting | bytes 17825792
  410.6 298.8 %while.15 = (s32[]{:T(128)}, f32[4,544]{1,0:T(4,128)S(1)}, f32[4,544]{1,0:T(4,128)S(1)}, f32[544,4,64]{0,2,1:T(8,128)S(1)}, bf16[34,512,4,64]{1,3,2,0:T(8,128)(2...) while((s32[]{:T(128)}, f32[4,544]{1,0:T(4,128)S(1)}, ...), condition=%wide.region_4.5_spmd.clone, body=%wide.region_1.4_spmd.clone.sunk | while | flops 294556416 | bytes 33252484 | solution.py:79
  410.6 3.8 bitcast_reduce_fusion.2
  419.4 3.8 bitcast_reduce_fusion.2
  428.2 3.8 bitcast_reduce_fusion.2
  437.0 3.8 bitcast_reduce_fusion.2
  445.8 3.8 bitcast_reduce_fusion.2
  454.6 3.8 bitcast_reduce_fusion.2
  463.4 3.8 bitcast_reduce_fusion.2
  472.2 3.8 bitcast_reduce_fusion.2
  480.9 3.8 bitcast_reduce_fusion.2
  498.5 3.8 bitcast_reduce_fusion.2
  507.3 3.8 bitcast_reduce_fusion.2
  516.1 3.8 bitcast_reduce_fusion.2
  524.9 3.8 bitcast_reduce_fusion.2
  533.7 3.8 bitcast_reduce_fusion.2
  542.4 3.8 bitcast_reduce_fusion.2
  551.2 3.8 bitcast_reduce_fusion.2
  560.0 3.8 bitcast_reduce_fusion.2
  568.8 3.8 bitcast_reduce_fusion.2
  577.6 3.8 bitcast_reduce_fusion.2
  586.4 3.8 bitcast_reduce_fusion.2
  595.2 3.8 bitcast_reduce_fusion.2
  603.9 3.8 bitcast_reduce_fusion.2
  612.7 3.8 bitcast_reduce_fusion.2
  621.5 3.8 bitcast_reduce_fusion.2
  630.3 3.8 bitcast_reduce_fusion.2
  639.1 3.8 bitcast_reduce_fusion.2
  647.9 3.8 bitcast_reduce_fusion.2
  656.7 3.8 bitcast_reduce_fusion.2
  665.4 3.8 bitcast_reduce_fusion.2
  674.2 3.8 bitcast_reduce_fusion.2
  683.0 3.8 bitcast_reduce_fusion.2
  691.8 3.8 bitcast_reduce_fusion.2
  700.6 3.8 bitcast_reduce_fusion.2
  712.8 9.5 %all-gather.1 = bf16[4,2,1024]{2,1,0:T(2,128)(2,1)S(1)} all-gather(bf16[1,2,1024]{2,1,0:T(2,128)(2,1)S(1)} %bitcast.85), channel_id=1, replica_groups=mesh['seq'=32,'type'=4] {'type'}, dimensions={0}, use_global_device_ids=true | all-gather | bytes 20480 | tf_op jit(solution)/shard_map/all_gather | solution.py:106
  722.4 7.4 all_gather.19
  729.9 20.7 %reduce-scatter.2.cloned.1.call-done = f32[136,1024]{1,0:T(8,128)} async-done(((f32[544,1024]{1,0:T(8,128)}), f32[136,1024]{1,0:T(8,128)}) %reduce-scatter.2.cloned.1.call-update) | async-done | bytes 557072 | tf_op jit(solution)/shard_map/reduce_scatter | solution.py:84
  752.6 109.4 %all-gather.8.cloned.1.call-done = bf16[8,1024,1024]{2,1,0:T(8,128)(2,1)} async-done(((bf16[2,1024,1024]{2,1,0:T(8,128)(2,1)}), bf16[8,1024,1024]{2,1,0:T(8,128)(2,1)}) %all-gather.8.cloned.1.call-update) | async-done | bytes 16777232 | tf_op jit(solution)/shard_map/all_gather | solution.py:105
  862.1 7.6 fusion.32
  (297 shorter events, 186.5 us)
Async XLA Ops:
  7.2 28.8 %copy-start = (bf16[3,1024,256]{2,1,0:T(8,128)(2,1)S(1)}, bf16[3,1024,256]{2,1,0:T(8,128)(2,1)}, u32[]{:S(2)}) copy-start(bf16[3,1024,256]{2,1,0:T(8,128)(2,1)} %param.16) | copy-start | bytes 4718596
  7.2 28.7 %all-gather.6.cloned.1.call-start = ((), (), s32[]{:S(2)}) async-start(), calls=%async_computation.2 | async-start | bytes 1392640 | tf_op jit(solution)/shard_map/all_gather | solution.py:50
  11.0 348.0 %all-gather.10.cloned.1.call-start = ((), (), s32[]{:S(2)}) async-start(), calls=%async_computation.5 | async-start | bytes 9191424 | tf_op jit(solution)/shard_map/all_gather | solution.py:67
  43.4 152.4 %all-to-all-start = ((bf16[32,544,256]{2,1,0:T(8,128)(2,1)}), bf16[32,544,256]{2,1,0:T(8,128)(2,1)}, u32[]{:S(2)}, u32[]{:S(2)}) async-start(bf16[32,544,256]{2,1,0:T(8,128)(2,1)} %stack.3), calls=%async_computation | async-start | bytes 17825792 | tf_op jit(solution)/shard_map/all_to_all | solution.py:70
  50.5 700.1 %reduce-scatter.2.cloned.1.call-start = ((), (), s32[]{:S(2)}) async-start(), calls=%async_computation.3 | async-start | bytes 2785280 | tf_op jit(solution)/shard_map/reduce_scatter | solution.py:84
  410.6 298.8 %copy-start.5 = (bf16[256,1024]{1,0:T(8,128)(2,1)S(1)}, bf16[256,1024]{1,0:T(8,128)(2,1)}, u32[]{:S(2)}) copy-start(bf16[256,1024]{1,0:T(8,128)(2,1)} %param.17) | copy-start | bytes 1572868
  414.4 3.7 copy-start.2
  423.2 3.7 copy-start.2
  432.0 3.7 copy-start.2
  440.8 3.7 copy-start.2
  449.6 3.7 copy-start.2
  458.4 3.7 copy-start.2
  467.1 3.7 copy-start.2
  475.9 3.7 copy-start.2
  484.7 3.7 copy-start.2
  493.5 3.7 copy-start.2
  502.3 3.7 copy-start.2
  511.1 3.7 copy-start.2
  519.9 3.7 copy-start.2
  528.6 3.7 copy-start.2
  537.4 3.7 copy-start.2
  546.2 3.7 copy-start.2
  555.0 3.7 copy-start.2
  563.8 3.7 copy-start.2
  572.6 3.7 copy-start.2
  581.4 3.7 copy-start.2
  590.1 3.7 copy-start.2
  598.9 3.7 copy-start.2
  607.7 3.7 copy-start.2
  616.5 3.7 copy-start.2
  625.3 3.7 copy-start.2
  634.1 3.7 copy-start.2
  642.9 3.7 copy-start.2
  651.6 3.7 copy-start.2
  660.4 3.7 copy-start.2
  669.2 3.7 copy-start.2
  678.0 3.7 copy-start.2
  686.8 3.7 copy-start.2
  695.6 3.7 copy-start.2
  704.4 3.7 copy-start.2
  709.5 3.4 copy-start.10
  709.5 12.9 %copy-start.6 = (bf16[2,1024,16]{1,2,0:T(8,128)(2,1)S(1)}, bf16[2,1024,16]{1,2,0:T(8,128)(2,1)}, u32[]{:S(2)}) copy-start(bf16[2,1024,16]{1,2,0:T(8,128)(2,1)} %param.21) | copy-start | bytes 196612
  709.5 41.1 %copy-start.3 = (bf16[136,1024]{1,0:T(8,128)(2,1)S(1)}, bf16[136,1024]{1,0:T(8,128)(2,1)}, u32[]{:S(2)}) copy-start(bf16[136,1024]{1,0:T(8,128)(2,1)} %param.12) | copy-start | bytes 835588
  709.5 41.1 %copy-start.8 = (f32[1024]{0:T(1024)S(1)}, f32[1024]{0:T(1024)}, u32[]{:S(2)}) copy-start(f32[1024]{0:T(1024)} %param.14) | copy-start | bytes 12292
  711.4 40.5 %copy-start.9 = (f32[1024]{0:T(1024)S(1)}, f32[1024]{0:T(1024)}, u32[]{:S(2)}) copy-start(f32[1024]{0:T(1024)} %param.15) | copy-start | bytes 12292
  711.4 150.7 %all-gather.8.cloned.1.call-start = ((), (), s32[]{:S(2)}) async-start(), calls=%async_computation.4 | async-start | bytes 20971520 | tf_op jit(solution)/shard_map/all_gather | solution.py:105
  751.9 117.8 %copy-start.4 = (bf16[136,1024]{1,0:T(8,128)(2,1)}, bf16[136,1024]{1,0:T(8,128)(2,1)S(1)}, u32[]{:S(2)}) copy-start(bf16[136,1024]{1,0:T(8,128)(2,1)S(1)} %get-tuple-element.104) | copy-start | bytes 835588
  862.1 8.6 copy-start.1
  (1 other events, 2.5 us)
Sparse Core Ops, SparseCore 0:
  11.1 24.7 all-gather.5
  39.1 319.8 all-gather.9
  711.5 39.0 reduce-scatter.1
  752.2 109.7 all-gather.7
